TPU v7x, 128 devices: a whole 4x4x4 slice. The times are simulated.
128 devices in a mesh: grid: 32 (over y, x, core), layer: 4 (over z).
Axes of the slice: x: 4, y: 4, z: 4, core: 2. Of those that a mesh axis runs over, the one named last changes fastest.
Arguments:
- h_blocks: bfloat16 [1024, 8, 128, 128], P('grid', 'layer'), may hold values from -0.09375 to 0.09375
- block_cols: int32 [1024, 8], P('grid', 'layer'), may hold values from 0 to 1023, as said below
- t_now: bfloat16 [131072, 1536], P(('grid', 'layer')), may hold values from -6 to 6
- t_prev: bfloat16 [131072, 1536], P(('grid', 'layer')), may hold values from -6 to 6
Outputs:
- next_term: bfloat16 [131072, 1536], P(('grid', 'layer'))
- after_term: bfloat16 [131072, 1536], P(('grid', 'layer'))
Inputs may be any that keep to these rules, and one draw needn't show every extreme that they name: block_cols[i, 0] = i. With g = i // 32, every block column lies among the block rows g * 32 - 2 to g * 32 + 33 counted cyclically modulo 1024, and both ends of that range are named in every block row.
All inputs are finite; a program needn't handle non-finite values.
Results may differ from a plain program's by a relative error of at most 0.019.
Values may be sent and summed in bfloat16 or wider, within the bound.
No kernel may reach another device: no remote copies, remote signals or barrier semaphores. Data moves between devices by JAX's collectives and lax.ppermute only.
A program may use at most 192 MiB of HBM per device.

v0:
```python
import jax
import jax.numpy as jnp
from jax import lax
from jax.sharding import PartitionSpec as P

KB = 8
HB = 2
NCH = 4


def padded(array, width):
    size, length = (lax.axis_size("grid"), array.shape[0])
    up = [(i, (i + 1) % size) for i in range(size)]
    down = [(j, i) for i, j in up]
    before = lax.ppermute(array[length - width :], "grid", up)
    after = lax.ppermute(array[:width], "grid", down)
    return jnp.concatenate([before, array, after], axis=0)


def own_rows(h_own, rel_own, chunk):
    block_size = h_own.shape[2]
    panel = lax.all_gather(chunk, "layer", axis=0, tiled=True)
    wide = padded(panel, HB * block_size)
    blocks = wide.reshape(wide.shape[0] // block_size, block_size, chunk.shape[1])
    picked = blocks[rel_own]
    acc = jnp.einsum("rsij,rsjc->ric", h_own, picked, preferred_element_type=jnp.float32)
    return acc.reshape(chunk.shape[0], chunk.shape[1])


def shards(h_blocks, block_cols, t_now, t_prev):
    group_rows = h_blocks.shape[0]
    total_blocks = group_rows * lax.axis_size("grid")
    first_block = lax.axis_index("grid") * group_rows
    relative = (block_cols - first_block + HB + total_blocks) % total_blocks
    h_own = lax.all_to_all(h_blocks, "layer", 0, 1, tiled=True)
    rel_own = lax.all_to_all(relative, "layer", 0, 1, tiled=True)
    width = t_now.shape[1]
    step = width // NCH

    def recur(current, previous):
        outs = []
        for c in range(NCH):
            acc = own_rows(h_own, rel_own, current[c])
            outs.append((2.0 * acc - previous[c].astype(jnp.float32)).astype(jnp.bfloat16))
        return outs

    now_chunks = [t_now[:, c * step : (c + 1) * step] for c in range(NCH)]
    prev_chunks = [t_prev[:, c * step : (c + 1) * step] for c in range(NCH)]
    next_chunks = recur(now_chunks, prev_chunks)
    after_chunks = recur(next_chunks, now_chunks)
    return (jnp.concatenate(next_chunks, axis=1), jnp.concatenate(after_chunks, axis=1))


def solution(mesh):
    in_specs = (
        P("grid", "layer", None, None),
        P("grid", "layer"),
        P(("grid", "layer"), None),
        P(("grid", "layer"), None),
    )
    out_specs = (P(("grid", "layer"), None), P(("grid", "layer"), None))
    return jax.shard_map(shards, mesh=mesh, in_specs=in_specs, out_specs=out_specs, check_vma=False)
```

profile of v0, /device:TPU:0, one launch (start us, length us, event | category | flops | bytes accessed | tf_op | source)
XLA Modules:
  0.0 535.9 jit_solution(12677658248927611347)
XLA Ops:
  13.1 10.5 %all_to_all.37 = s32[4,8,2]{1,2,0:T(2,128)S(1)} all-to-all(s32[4,8,2]{1,2,0:T(2,128)S(1)} %copy.9), channel_id=1, replica_groups=mesh['grid'=32,'layer'=4] {'layer'}, dimensions={0} | all-to-all | bytes 512 | tf_op jit(solution)/shard_map/all_to_all | solution.py:36
  27.4 48.1 %all-to-all-done.1 = bf16[32,2,128,128]{3,2,1,0:T(8,128)(2,1)S(1)} async-done(((bf16[32,2,128,128]{3,2,1,0:T(8,128)(2,1)}), bf16[32,2,128,128]{3,2,1,0:T(8,128)(2,1)S(1)}, u32[]{:S(2)}, u32[]{:S(2)}) %all-to-all-start.1) | async-done | bytes 2097184 | tf_op jit(solution)/shard_map/all_to_all | solution.py:35
  84.8 32.1 %all-gather.13.cloned.1.call-done = bf16[4096,384]{1,0:T(8,128)(2,1)} async-done(((bf16[1024,384]{1,0:T(8,128)(2,1)}), bf16[4096,384]{1,0:T(8,128)(2,1)}) %all-gather.13.cloned.1.call-update) | async-done | bytes 3145744 | tf_op jit(solution)/shard_map/all_gather | solution.py:22
  118.8 5.1 collective-permute-start.5
  123.8 34.6 %all-gather.11.cloned.1.call-done = bf16[4096,384]{1,0:T(8,128)(2,1)} async-done(((bf16[1024,384]{1,0:T(8,128)(2,1)}), bf16[4096,384]{1,0:T(8,128)(2,1)}) %all-gather.11.cloned.1.call-update) | async-done | bytes 3145744 | tf_op jit(solution)/shard_map/all_gather | solution.py:22
  160.2 40.0 %all-gather.9.cloned.1.call-done = bf16[4096,384]{1,0:T(8,128)(2,1)} async-done(((bf16[1024,384]{1,0:T(8,128)(2,1)}), bf16[4096,384]{1,0:T(8,128)(2,1)}) %all-gather.9.cloned.1.call-update) | async-done | bytes 3145744 | tf_op jit(solution)/shard_map/all_gather | solution.py:22
  206.2 7.1 %pad_maximum_fusion.3 = bf16[4608,384]{1,0:T(8,128)(2,1)} fusion(bf16[256,384]{1,0:T(8,128)(2,1)S(1)} %collective-permute-done.7, bf16[4096,384]{1,0:T(8,128)(2,1)} %all-gather.15.cloned.1.call-done, bf16[256,384]{1,0:T(8,128)(2,1)S(1)} %collective-permute-done.6), kind=kLoop, calls=%fused_computation.11 | loop fusion | flops 10616832 | bytes 7077888 | tf_op jit(solution)/shard_map/concatenate | solution.py:17
  213.3 6.1 %gather_fusion.3 = bf16[64,128,384]{2,1,0:T(8,128)(2,1)} fusion(bf16[36,128,384]{2,1,0:T(8,128)(2,1)} %bitcast.132, s32[1024]{0:T(1024)S(1)} %pad_clamp_fusion), kind=kCustom, calls=%fused_computation.3 | custom fusion | bytes 12583168 | tf_op jit(solution)/shard_map/gather | solution.py:25
  219.4 5.6 %collective-permute-start.1 = (bf16[256,384]{1,0:T(8,128)(2,1)S(1)}, bf16[256,384]{1,0:T(8,128)(2,1)S(1)}, u32[]{:S(2)}, u32[]{:S(2)}) collective-permute-start(bf16[256,384]{1,0:T(8,128)(2,1)S(1)} %copy-done.16), channel_id=1, source_target_pairs={{4,0},{8,4},{12,8},{16,12},{20,16},{24,20},{28,24},{32,28},{36,32}... | collective-permute-start | bytes 589832 | tf_op jit(solution)/shard_map/ppermute | solution.py:16
  224.9 7.0 %pad_maximum_fusion.2 = bf16[4608,384]{1,0:T(8,128)(2,1)} fusion(bf16[256,384]{1,0:T(8,128)(2,1)S(1)} %collective-permute-done.5, bf16[4096,384]{1,0:T(8,128)(2,1)} %all-gather.13.cloned.1.call-done, bf16[256,384]{1,0:T(8,128)(2,1)S(1)} %collective-permute-done.4), kind=kLoop, calls=%fused_computation.10 | loop fusion | flops 10616832 | bytes 7077888 | tf_op jit(solution)/shard_map/concatenate | solution.py:17
  232.0 6.1 %gather_fusion.2 = bf16[64,128,384]{2,1,0:T(8,128)(2,1)} fusion(bf16[36,128,384]{2,1,0:T(8,128)(2,1)} %bitcast.133, s32[1024]{0:T(1024)S(1)} %pad_clamp_fusion), kind=kCustom, calls=%fused_computation.2 | custom fusion | bytes 12583168 | tf_op jit(solution)/shard_map/gather | solution.py:25
  238.1 5.3 bitcast_multiply_fusion.4
  245.9 6.3 %pad_maximum_fusion.1 = bf16[4608,384]{1,0:T(8,128)(2,1)} fusion(bf16[256,384]{1,0:T(8,128)(2,1)S(1)} %collective-permute-done.3, bf16[4096,384]{1,0:T(8,128)(2,1)S(1)} %copy-done.11, bf16[256,384]{1,0:T(8,128)(2,1)S(1)} %collective-permute-done.2), kind=kLoop, calls=%fused_computation.9 | loop fusion | flops 10616832 | bytes 7077888 | tf_op jit(solution)/shard_map/concatenate | solution.py:17
  252.2 6.1 %gather_fusion.1 = bf16[64,128,384]{2,1,0:T(8,128)(2,1)} fusion(bf16[36,128,384]{2,1,0:T(8,128)(2,1)} %bitcast.134, s32[1024]{0:T(1024)S(1)} %pad_clamp_fusion), kind=kCustom, calls=%fused_computation.1 | custom fusion | bytes 12583168 | tf_op jit(solution)/shard_map/gather | solution.py:25
  258.3 5.3 bitcast_multiply_fusion.6
  263.6 6.5 %pad_maximum_fusion = bf16[4608,384]{1,0:T(8,128)(2,1)} fusion(bf16[256,384]{1,0:T(8,128)(2,1)S(1)} %collective-permute-done.1, bf16[4096,384]{1,0:T(8,128)(2,1)S(1)} %copy-done.10, bf16[256,384]{1,0:T(8,128)(2,1)S(1)} %collective-permute-done), kind=kLoop, calls=%fused_computation.8 | loop fusion | flops 10616832 | bytes 7077888 | tf_op jit(solution)/shard_map/concatenate | solution.py:17
  270.1 6.1 %gather_fusion = bf16[64,128,384]{2,1,0:T(8,128)(2,1)} fusion(bf16[36,128,384]{2,1,0:T(8,128)(2,1)} %bitcast.135, s32[1024]{0:T(1024)S(1)} %pad_clamp_fusion), kind=kCustom, calls=%fused_computation | custom fusion | bytes 12583168 | tf_op jit(solution)/shard_map/gather | solution.py:25
  288.6 29.9 %all-gather.23.cloned.1.call-done = bf16[4096,384]{1,0:T(8,128)(2,1)} async-done(((bf16[1024,384]{1,0:T(8,128)(2,1)}), bf16[4096,384]{1,0:T(8,128)(2,1)}) %all-gather.23.cloned.1.call-update) | async-done | bytes 3145744 | tf_op jit(solution)/shard_map/all_gather | solution.py:22
  324.7 35.1 %all-gather.21.cloned.1.call-done = bf16[4096,384]{1,0:T(8,128)(2,1)} async-done(((bf16[1024,384]{1,0:T(8,128)(2,1)}), bf16[4096,384]{1,0:T(8,128)(2,1)}) %all-gather.21.cloned.1.call-update) | async-done | bytes 3145744 | tf_op jit(solution)/shard_map/all_gather | solution.py:22
  366.7 34.6 %all-gather.19.cloned.1.call-done = bf16[4096,384]{1,0:T(8,128)(2,1)} async-done(((bf16[1024,384]{1,0:T(8,128)(2,1)}), bf16[4096,384]{1,0:T(8,128)(2,1)}) %all-gather.19.cloned.1.call-update) | async-done | bytes 3145744 | tf_op jit(solution)/shard_map/all_gather | solution.py:22
  403.1 40.2 %all-gather.17.cloned.1.call-done = bf16[4096,384]{1,0:T(8,128)(2,1)} async-done(((bf16[1024,384]{1,0:T(8,128)(2,1)}), bf16[4096,384]{1,0:T(8,128)(2,1)}) %all-gather.17.cloned.1.call-update) | async-done | bytes 3145744 | tf_op jit(solution)/shard_map/all_gather | solution.py:22
  449.2 7.1 %pad_maximum_fusion.7 = bf16[4608,384]{1,0:T(8,128)(2,1)} fusion(bf16[256,384]{1,0:T(8,128)(2,1)S(1)} %collective-permute-done.15, bf16[4096,384]{1,0:T(8,128)(2,1)} %all-gather.23.cloned.1.call-done, bf16[256,384]{1,0:T(8,128)(2,1)S(1)} %collective-permute-done.14), kind=kLoop, calls=%fused_computation.15 | loop fusion | flops 10616832 | bytes 7077888 | tf_op jit(solution)/shard_map/concatenate | solution.py:17
  456.3 6.1 %gather_fusion.7 = bf16[64,128,384]{2,1,0:T(8,128)(2,1)} fusion(bf16[36,128,384]{2,1,0:T(8,128)(2,1)} %bitcast.136, s32[1024]{0:T(1024)S(1)} %pad_clamp_fusion), kind=kCustom, calls=%fused_computation.7 | custom fusion | bytes 12583168 | tf_op jit(solution)/shard_map/gather | solution.py:25
  462.3 5.4 %bitcast_multiply_fusion = f32[8,384,128]{1,2,0:T(8,128)} fusion(bf16[8,8,128,128]{3,2,1,0:T(8,128)(2,1)S(1)} %bitcast.119, bf16[8,8,128,384]{3,2,1,0:T(8,128)(2,1)} %bitcast.128), kind=kOutput, calls=%fused_computation.34 | convolution fusion | flops 805699584 | bytes 9961472 | tf_op jit(solution)/shard_map/rsij,rsjc->ric/dot_general | solution.py:26
  472.8 6.5 %pad_maximum_fusion.6 = bf16[4608,384]{1,0:T(8,128)(2,1)} fusion(bf16[256,384]{1,0:T(8,128)(2,1)S(1)} %collective-permute-done.13, bf16[4096,384]{1,0:T(8,128)(2,1)S(1)} %copy-done.14, bf16[256,384]{1,0:T(8,128)(2,1)S(1)} %collective-permute-done.12), kind=kLoop, calls=%fused_computation.14 | loop fusion | flops 10616832 | bytes 7077888 | tf_op jit(solution)/shard_map/concatenate | solution.py:17
  479.2 6.1 %gather_fusion.6 = bf16[64,128,384]{2,1,0:T(8,128)(2,1)} fusion(bf16[36,128,384]{2,1,0:T(8,128)(2,1)} %bitcast.137, s32[1024]{0:T(1024)S(1)} %pad_clamp_fusion), kind=kCustom, calls=%fused_computation.6 | custom fusion | bytes 12583168 | tf_op jit(solution)/shard_map/gather | solution.py:25
  485.3 5.4 %bitcast_multiply_fusion.1 = f32[8,384,128]{1,2,0:T(8,128)} fusion(bf16[8,8,128,128]{3,2,1,0:T(8,128)(2,1)S(1)} %bitcast.120, bf16[8,8,128,384]{3,2,1,0:T(8,128)(2,1)} %bitcast.129), kind=kOutput, calls=%fused_computation.35 | convolution fusion | flops 805699584 | bytes 9961472 | tf_op jit(solution)/shard_map/rsij,rsjc->ric/dot_general | solution.py:26
  490.7 6.3 %pad_maximum_fusion.5 = bf16[4608,384]{1,0:T(8,128)(2,1)} fusion(bf16[256,384]{1,0:T(8,128)(2,1)S(1)} %collective-permute-done.11, bf16[4096,384]{1,0:T(8,128)(2,1)S(1)} %copy-done.13, bf16[256,384]{1,0:T(8,128)(2,1)S(1)} %collective-permute-done.10), kind=kLoop, calls=%fused_computation.13 | loop fusion | flops 10616832 | bytes 7077888 | tf_op jit(solution)/shard_map/concatenate | solution.py:17
  497.0 6.1 %gather_fusion.5 = bf16[64,128,384]{2,1,0:T(8,128)(2,1)} fusion(bf16[36,128,384]{2,1,0:T(8,128)(2,1)} %bitcast.138, s32[1024]{0:T(1024)S(1)} %pad_clamp_fusion), kind=kCustom, calls=%fused_computation.5 | custom fusion | bytes 12583168 | tf_op jit(solution)/shard_map/gather | solution.py:25
  503.0 5.3 bitcast_multiply_fusion.2
  508.4 6.5 %pad_maximum_fusion.4 = bf16[4608,384]{1,0:T(8,128)(2,1)} fusion(bf16[256,384]{1,0:T(8,128)(2,1)S(1)} %collective-permute-done.9, bf16[4096,384]{1,0:T(8,128)(2,1)S(1)} %copy-done.12, bf16[256,384]{1,0:T(8,128)(2,1)S(1)} %collective-permute-done.8), kind=kLoop, calls=%fused_computation.12 | loop fusion | flops 10616832 | bytes 7077888 | tf_op jit(solution)/shard_map/concatenate | solution.py:17
  514.9 6.1 %gather_fusion.4 = bf16[64,128,384]{2,1,0:T(8,128)(2,1)} fusion(bf16[36,128,384]{2,1,0:T(8,128)(2,1)} %bitcast.131, s32[1024]{0:T(1024)S(1)} %pad_clamp_fusion), kind=kCustom, calls=%fused_computation.4 | custom fusion | bytes 12583168 | tf_op jit(solution)/shard_map/gather | solution.py:25
  (110 shorter events, 76.9 us)
Async XLA Ops:
  7.2 5.8 %copy-start.18 = (s32[32,2]{0,1:T(2,128)S(1)}, s32[32,2]{0,1:T(2,128)}, u32[]{:S(2)}) copy-start(s32[32,2]{0,1:T(2,128)} %param.5) | copy-start | bytes 772
  7.2 71.4 %all-gather.15.cloned.1.call-start = ((), (), s32[]{:S(2)}) async-start(), calls=%async_computation.5 | async-start | bytes 3932160 | tf_op jit(solution)/shard_map/all_gather | solution.py:22
  10.9 106.1 %all-gather.13.cloned.1.call-start = ((), (), s32[]{:S(2)}) async-start(), calls=%async_computation.4 | async-start | bytes 3932160 | tf_op jit(solution)/shard_map/all_gather | solution.py:22
  11.6 146.8 %all-gather.11.cloned.1.call-start = ((), (), s32[]{:S(2)}) async-start(), calls=%async_computation.3 | async-start | bytes 3932160 | tf_op jit(solution)/shard_map/all_gather | solution.py:22
  12.4 187.9 %all-gather.9.cloned.1.call-start = ((), (), s32[]{:S(2)}) async-start(), calls=%async_computation.2 | async-start | bytes 3932160 | tf_op jit(solution)/shard_map/all_gather | solution.py:22
  23.6 52.0 %all-to-all-start.1 = ((bf16[32,2,128,128]{3,2,1,0:T(8,128)(2,1)}), bf16[32,2,128,128]{3,2,1,0:T(8,128)(2,1)S(1)}, u32[]{:S(2)}, u32[]{:S(2)}) async-start(bf16[32,2,128,128]{3,2,1,0:T(8,128)(2,1)} %param.4), calls=%async_computation.1 | async-start | bytes 4194304 | tf_op jit(solution)/shard_map/all_to_all | solution.py:35
  27.2 291.3 %all-gather.23.cloned.1.call-start = ((), (), s32[]{:S(2)}) async-start(), calls=%async_computation.9 | async-start | bytes 3932160 | tf_op jit(solution)/shard_map/all_gather | solution.py:22
  79.7 122.4 %collective-permute-start.6 = (bf16[256,384]{1,0:T(8,128)(2,1)S(1)}, bf16[256,384]{1,0:T(8,128)(2,1)S(1)}, u32[]{:S(2)}, u32[]{:S(2)}) collective-permute-start(bf16[256,384]{1,0:T(8,128)(2,1)S(1)} %get-tuple-element.28), channel_id=1, source_target_pairs={{0,4},{4,8},{8,12},{12,16},{16,20},{20,24},{24,28},{28,32},{32,36}... | collective-permute-start | bytes 589832 | tf_op jit(solution)/shard_map/ppermute | solution.py:15
  79.8 126.4 %collective-permute-start.7 = (bf16[256,384]{1,0:T(8,128)(2,1)S(1)}, bf16[256,384]{1,0:T(8,128)(2,1)S(1)}, u32[]{:S(2)}, u32[]{:S(2)}) collective-permute-start(bf16[256,384]{1,0:T(8,128)(2,1)S(1)} %get-tuple-element.29), channel_id=1, source_target_pairs={{4,0},{8,4},{12,8},{16,12},{20,16},{24,20},{28,24},{32,28},{36,32}... | collective-permute-start | bytes 589832 | tf_op jit(solution)/shard_map/ppermute | solution.py:16
  118.8 100.6 %collective-permute-start.4 = (bf16[256,384]{1,0:T(8,128)(2,1)}, bf16[256,384]{1,0:T(8,128)(2,1)S(1)}, u32[]{:S(2)}, u32[]{:S(2)}) collective-permute-start(bf16[256,384]{1,0:T(8,128)(2,1)} %get-tuple-element.26), channel_id=1, source_target_pairs={{0,4},{4,8},{8,12},{12,16},{16,20},{20,24},{24,28},{28,32},{32,36}... | collective-permute-start | bytes 589832 | tf_op jit(solution)/shard_map/ppermute | solution.py:15
  118.8 106.2 %collective-permute-start.5 = (bf16[256,384]{1,0:T(8,128)(2,1)}, bf16[256,384]{1,0:T(8,128)(2,1)S(1)}, u32[]{:S(2)}, u32[]{:S(2)}) collective-permute-start(bf16[256,384]{1,0:T(8,128)(2,1)} %get-tuple-element.27), channel_id=1, source_target_pairs={{4,0},{8,4},{12,8},{16,12},{20,16},{24,20},{28,24},{32,28},{36,32}... | collective-permute-start | bytes 589832 | tf_op jit(solution)/shard_map/ppermute | solution.py:16
  160.2 85.7 %collective-permute-start.2 = (bf16[256,384]{1,0:T(8,128)(2,1)}, bf16[256,384]{1,0:T(8,128)(2,1)S(1)}, u32[]{:S(2)}, u32[]{:S(2)}) collective-permute-start(bf16[256,384]{1,0:T(8,128)(2,1)} %get-tuple-element.24), channel_id=1, source_target_pairs={{0,4},{4,8},{8,12},{12,16},{16,20},{20,24},{24,28},{28,32},{32,36}... | collective-permute-start | bytes 589832 | tf_op jit(solution)/shard_map/ppermute | solution.py:15
  202.1 43.9 %collective-permute-start.3 = (bf16[256,384]{1,0:T(8,128)(2,1)}, bf16[256,384]{1,0:T(8,128)(2,1)S(1)}, u32[]{:S(2)}, u32[]{:S(2)}) collective-permute-start(bf16[256,384]{1,0:T(8,128)(2,1)} %get-tuple-element.25), channel_id=1, source_target_pairs={{4,0},{8,4},{12,8},{16,12},{20,16},{24,20},{28,24},{32,28},{36,32}... | collective-permute-start | bytes 589832 | tf_op jit(solution)/shard_map/ppermute | solution.py:16
  206.2 57.4 %collective-permute-start = (bf16[256,384]{1,0:T(8,128)(2,1)}, bf16[256,384]{1,0:T(8,128)(2,1)S(1)}, u32[]{:S(2)}, u32[]{:S(2)}) collective-permute-start(bf16[256,384]{1,0:T(8,128)(2,1)} %get-tuple-element.18), channel_id=1, source_target_pairs={{0,4},{4,8},{8,12},{12,16},{16,20},{20,24},{24,28},{28,32},{32,36}... | collective-permute-start | bytes 589832 | tf_op jit(solution)/shard_map/ppermute | solution.py:15
  213.3 6.1 %copy-start.16 = (bf16[256,384]{1,0:T(8,128)(2,1)S(1)}, bf16[256,384]{1,0:T(8,128)(2,1)}, u32[]{:S(2)}) copy-start(bf16[256,384]{1,0:T(8,128)(2,1)} %get-tuple-element.19) | copy-start | bytes 589828
  219.4 44.2 %collective-permute-start.1 = (bf16[256,384]{1,0:T(8,128)(2,1)S(1)}, bf16[256,384]{1,0:T(8,128)(2,1)S(1)}, u32[]{:S(2)}, u32[]{:S(2)}) collective-permute-start(bf16[256,384]{1,0:T(8,128)(2,1)S(1)} %copy-done.16), channel_id=1, source_target_pairs={{4,0},{8,4},{12,8},{16,12},{20,16},{24,20},{28,24},{32,28},{36,32}... | collective-permute-start | bytes 589832 | tf_op jit(solution)/shard_map/ppermute | solution.py:16
  258.3 5.4 copy-start.10
  283.5 76.3 %all-gather.21.cloned.1.call-start = ((), (), s32[]{:S(2)}) async-start(), calls=%async_computation.8 | async-start | bytes 3932160 | tf_op jit(solution)/shard_map/all_gather | solution.py:22
  284.1 117.2 %all-gather.19.cloned.1.call-start = ((), (), s32[]{:S(2)}) async-start(), calls=%async_computation.7 | async-start | bytes 3932160 | tf_op jit(solution)/shard_map/all_gather | solution.py:22
  284.8 158.4 %all-gather.17.cloned.1.call-start = ((), (), s32[]{:S(2)}) async-start(), calls=%async_computation.6 | async-start | bytes 3932160 | tf_op jit(solution)/shard_map/all_gather | solution.py:22
  319.6 125.5 %collective-permute-start.14 = (bf16[256,384]{1,0:T(8,128)(2,1)S(1)}, bf16[256,384]{1,0:T(8,128)(2,1)S(1)}, u32[]{:S(2)}, u32[]{:S(2)}) collective-permute-start(bf16[256,384]{1,0:T(8,128)(2,1)S(1)} %get-tuple-element.12), channel_id=1, source_target_pairs={{0,4},{4,8},{8,12},{12,16},{16,20},{20,24},{24,28},{28,32},{32,36}... | collective-permute-start | bytes 589832 | tf_op jit(solution)/shard_map/ppermute | solution.py:15
  319.7 129.5 %collective-permute-start.15 = (bf16[256,384]{1,0:T(8,128)(2,1)S(1)}, bf16[256,384]{1,0:T(8,128)(2,1)S(1)}, u32[]{:S(2)}, u32[]{:S(2)}) collective-permute-start(bf16[256,384]{1,0:T(8,128)(2,1)S(1)} %get-tuple-element.13), channel_id=1, source_target_pairs={{4,0},{8,4},{12,8},{16,12},{20,16},{24,20},{28,24},{32,28},{36,32}... | collective-permute-start | bytes 589832 | tf_op jit(solution)/shard_map/ppermute | solution.py:16
  361.6 106.1 %collective-permute-start.12 = (bf16[256,384]{1,0:T(8,128)(2,1)}, bf16[256,384]{1,0:T(8,128)(2,1)S(1)}, u32[]{:S(2)}, u32[]{:S(2)}) collective-permute-start(bf16[256,384]{1,0:T(8,128)(2,1)} %get-tuple-element.10), channel_id=1, source_target_pairs={{0,4},{4,8},{8,12},{12,16},{16,20},{20,24},{24,28},{28,32},{32,36}... | collective-permute-start | bytes 589832 | tf_op jit(solution)/shard_map/ppermute | solution.py:15
  361.6 111.1 %collective-permute-start.13 = (bf16[256,384]{1,0:T(8,128)(2,1)}, bf16[256,384]{1,0:T(8,128)(2,1)S(1)}, u32[]{:S(2)}, u32[]{:S(2)}) collective-permute-start(bf16[256,384]{1,0:T(8,128)(2,1)} %get-tuple-element.11), channel_id=1, source_target_pairs={{4,0},{8,4},{12,8},{16,12},{20,16},{24,20},{28,24},{32,28},{36,32}... | collective-permute-start | bytes 589832 | tf_op jit(solution)/shard_map/ppermute | solution.py:16
  403.1 87.6 %collective-permute-start.10 = (bf16[256,384]{1,0:T(8,128)(2,1)}, bf16[256,384]{1,0:T(8,128)(2,1)S(1)}, u32[]{:S(2)}, u32[]{:S(2)}) collective-permute-start(bf16[256,384]{1,0:T(8,128)(2,1)} %get-tuple-element.8), channel_id=1, source_target_pairs={{0,4},{4,8},{8,12},{12,16},{16,20},{20,24},{24,28},{28,32},{32,36}... | collective-permute-start | bytes 589832 | tf_op jit(solution)/shard_map/ppermute | solution.py:15
  445.0 45.6 %collective-permute-start.11 = (bf16[256,384]{1,0:T(8,128)(2,1)}, bf16[256,384]{1,0:T(8,128)(2,1)S(1)}, u32[]{:S(2)}, u32[]{:S(2)}) collective-permute-start(bf16[256,384]{1,0:T(8,128)(2,1)} %get-tuple-element.9), channel_id=1, source_target_pairs={{4,0},{8,4},{12,8},{16,12},{20,16},{24,20},{28,24},{32,28},{36,32}... | collective-permute-start | bytes 589832 | tf_op jit(solution)/shard_map/ppermute | solution.py:16
  449.2 59.2 %collective-permute-start.8 = (bf16[256,384]{1,0:T(8,128)(2,1)}, bf16[256,384]{1,0:T(8,128)(2,1)S(1)}, u32[]{:S(2)}, u32[]{:S(2)}) collective-permute-start(bf16[256,384]{1,0:T(8,128)(2,1)} %get-tuple-element.6), channel_id=1, source_target_pairs={{0,4},{4,8},{8,12},{12,16},{16,20},{20,24},{24,28},{28,32},{32,36}... | collective-permute-start | bytes 589832 | tf_op jit(solution)/shard_map/ppermute | solution.py:15
  462.3 5.4 %copy-start.17 = (bf16[256,384]{1,0:T(8,128)(2,1)S(1)}, bf16[256,384]{1,0:T(8,128)(2,1)}, u32[]{:S(2)}) copy-start(bf16[256,384]{1,0:T(8,128)(2,1)} %get-tuple-element.7) | copy-start | bytes 589828
  462.3 10.4 %copy-start.14 = (bf16[4096,384]{1,0:T(8,128)(2,1)S(1)}, bf16[4096,384]{1,0:T(8,128)(2,1)}, u32[]{:S(2)}) copy-start(bf16[4096,384]{1,0:T(8,128)(2,1)} %all-gather.21.cloned.1.call-done) | copy-start | bytes 9437188
  467.7 40.7 %collective-permute-start.9 = (bf16[256,384]{1,0:T(8,128)(2,1)S(1)}, bf16[256,384]{1,0:T(8,128)(2,1)S(1)}, u32[]{:S(2)}, u32[]{:S(2)}) collective-permute-start(bf16[256,384]{1,0:T(8,128)(2,1)S(1)} %copy-done.17), channel_id=1, source_target_pairs={{4,0},{8,4},{12,8},{16,12},{20,16},{24,20},{28,24},{32,28},{36,32}... | collective-permute-start | bytes 589832 | tf_op jit(solution)/shard_map/ppermute | solution.py:16
  485.3 5.4 %copy-start.13 = (bf16[4096,384]{1,0:T(8,128)(2,1)S(1)}, bf16[4096,384]{1,0:T(8,128)(2,1)}, u32[]{:S(2)}) copy-start(bf16[4096,384]{1,0:T(8,128)(2,1)} %all-gather.19.cloned.1.call-done) | copy-start | bytes 9437188
  503.0 5.4 copy-start.12
  (12 other events, 47.2 us)
Sparse Core Ops, SparseCore 0:
  11.0 64.1 all-gather.14
  76.8 40.1 all-gather.12
  118.6 39.7 all-gather.10
  160.5 39.7 all-gather.8
  283.6 34.8 all-gather.22
  320.0 39.7 all-gather.20
  361.5 39.7 all-gather.18
  403.5 39.7 all-gather.16
where the time goes:
time: 542 us; the launch traced here: 536 us
  waiting for transfers between devices  298 us (55%)
  local copies, waits for them, and re-layouts  70.3 us (13%)
  other arithmetic  61 us (11%)
  starting transfers between devices  43.2 us (8%)
  matrix products  37.6 us (7%)
  between operations  14.8 us (3%)
  blocking collectives  10.5 us (2%)
    all_gather x8, waiting for transfers between devices, own_rows(): panel = lax.all_gather(chunk, 'layer', axis=0, tiled=True)  246 us
    concatenate x8, other arithmetic, padded(): return jnp.concatenate([before, array, after], axis=0)  53.2 us
    gather x8, local copies, waits for them, and re-layouts, own_rows(): picked = blocks[rel_own]  48.5 us
    all_to_all x1, waiting for transfers between devices, shards(): h_own = lax.all_to_all(h_blocks, 'layer', 0, 1, tiled=True)  48.1 us
    ppermute x8, starting transfers between devices, padded(): after = lax.ppermute(array[:width], 'grid', down)  39.1 us
    dot_general x8, matrix products, own_rows(): jnp.einsum('rsij,rsjc->ric', h_own, picked, preferred_element_type=jnp.fl...  37.6 us
    slice x8, local copies, waits for them, and re-layouts, padded(): before = lax.ppermute(array[length - width:], 'grid', up)  13 us
  transfers between devices with their start and end apart: 25, of which 8 were waited for; matrix products, arithmetic and copies ran while one was open for 23% of the time, Pallas kernels for 0%

commit v1 on v0

--- a/solution.py
+++ b/solution.py
@@ -1,3 +1,4 @@
+import functools
 import jax
 import jax.numpy as jnp
 from jax import lax
@@ -6,6 +7,37 @@
 KB = 8
 HB = 2
 NCH = 4
+
+
+def joints_track(vec, in_dim):
+    tall = list(vec.shape[1:])
+    tall[in_dim] *= vec.shape[0]
+    return jnp.moveaxis(vec, 0, in_dim).reshape(tall)
+
+
+def _write_run(local_array, a_name, dimension_no):
+    n_axis = lax.psum(1, a_name)
+    pile = [(at, (at + 1) % n_axis) for at in range(n_axis)]
+    log = [(rr, src_i) for src_i, rr in pile]
+    piece_next, mixed_arr = ([], [])
+    for dev_j in [*range(n_axis - 1)]:
+        if dev_j % 2 == 0:
+            opened = lax.ppermute(piece_next[-1] if piece_next else local_array, a_name, perm=pile)
+            piece_next.append(opened)
+        else:
+            k_now = lax.ppermute(
+                mixed_arr[-1] if mixed_arr else local_array, axis_name=a_name, perm=log
+            )
+            mixed_arr.append(k_now)
+    odd = jnp.stack([*piece_next[::-1], local_array, *mixed_arr])
+    local_next = len(piece_next)
+    state_next = lax.axis_index(a_name)
+    raw_out = state_next - local_next
+    odd = odd[(jnp.arange(n_axis) - raw_out) % n_axis]
+    return joints_track(odd, dimension_no)
+
+
+bind_quarters_here = functools.partial(_write_run, a_name="layer", dimension_no=0)
 
 
 def padded(array, width):
@@ -19,7 +51,7 @@
 
 def own_rows(h_own, rel_own, chunk):
     block_size = h_own.shape[2]
-    panel = lax.all_gather(chunk, "layer", axis=0, tiled=True)
+    panel = bind_quarters_here(chunk)
     wide = padded(panel, HB * block_size)
     blocks = wide.reshape(wide.shape[0] // block_size, block_size, chunk.shape[1])
     picked = blocks[rel_own]

time: 542 us -> 500 us (0.923)
  waiting for transfers between devices: 298 us -> 147 us
  blocking collectives: 10.5 us -> 50.7 us
  local copies, waits for them, and re-layouts: 70.3 us -> 109 us
  starting transfers between devices: 43.2 us -> 68.6 us
  other arithmetic: 61 us -> 77.2 us
  between operations: 14.8 us -> 1.08 us
    all_gather x8 -> x0, waiting for transfers between devices: 246 us -> none  [own_rows(): panel = lax.all_gather(chunk, 'layer', axis=0, tiled=True)]
    ppermute x0 -> x24, waiting for transfers between devices: none -> 147 us  [the longest x16 120 us: _write_run(): lax.ppermute(piece_next[-1] if piece_next else local_array, a_name, perm=...]
    all_to_all x1, waiting for transfers between devices: 48.1 us -> 0.01 us  [shards(): h_own = lax.all_to_all(h_blocks, 'layer', 0, 1, tiled=True)]
    all_to_all x1, blocking collectives: 10.5 us -> 50.7 us  [shards(): rel_own = lax.all_to_all(relative, 'layer', 0, 1, tiled=True)]
    gather x0 -> x8, local copies, waits for them, and re-layouts: none -> 36.4 us  [_write_run(): odd = odd[(jnp.arange(n_axis) - raw_out) % n_axis]]
    another operation x0 -> x8, other arithmetic: none -> 24.9 us  [_write_run(): odd = jnp.stack([*piece_next[::-1], local_array, *mixed_arr])]
    ppermute x0 -> x24, starting transfers between devices: none -> 24.4 us  [the longest x8 18.9 us: _write_run(): lax.ppermute(mixed_arr[-1] if mixed_arr else local_array, axis_name=a_nam...]
    concatenate x8, other arithmetic: 53.2 us -> 44.9 us  [padded(): return jnp.concatenate([before, array, after], axis=0)]
  transfers between devices with their start and end apart: 25 -> 41, of which waited for: 8 -> 10; matrix products, arithmetic and copies ran while one was open for 23% -> 36% of each run, Pallas kernels for 0% -> 0%
where the time goes in v1:
time: 500 us; the launch traced here: 491 us
  waiting for transfers between devices  147 us (29%)
  local copies, waits for them, and re-layouts  109 us (22%)
  other arithmetic  77.2 us (15%)
  starting transfers between devices  68.6 us (14%)
  blocking collectives  50.7 us (10%)
  matrix products  37.7 us (8%)
    ppermute x16, waiting for transfers between devices, _write_run(): lax.ppermute(piece_next[-1] if piece_next else local_array, a_name, perm=...  120 us
    all_to_all x1, blocking collectives, shards(): rel_own = lax.all_to_all(relative, 'layer', 0, 1, tiled=True)  50.7 us
    gather x8, local copies, waits for them, and re-layouts, own_rows(): picked = blocks[rel_own]  48.5 us
    concatenate x8, other arithmetic, padded(): return jnp.concatenate([before, array, after], axis=0)  44.9 us
    ppermute x8, starting transfers between devices, padded(): after = lax.ppermute(array[:width], 'grid', down)  40.4 us
    dot_general x8, matrix products, own_rows(): jnp.einsum('rsij,rsjc->ric', h_own, picked, preferred_element_type=jnp.fl...  37.7 us
    gather x8, local copies, waits for them, and re-layouts, _write_run(): odd = odd[(jnp.arange(n_axis) - raw_out) % n_axis]  36.4 us
    ppermute x8, waiting for transfers between devices, _write_run(): lax.ppermute(mixed_arr[-1] if mixed_arr else local_array, axis_name=a_nam...  26.8 us
  transfers between devices with their start and end apart: 41, of which 10 were waited for; matrix products, arithmetic and copies ran while one was open for 36% of the time, Pallas kernels for 0%

profile of v1, /device:TPU:0, one launch (start us, length us, event | category | flops | bytes accessed | tf_op | source)
XLA Modules:
  0.0 490.8 jit_solution(12283766444547096611)
XLA Ops:
  11.1 16.9 %collective-permute-done.10 = bf16[1024,384]{1,0:T(8,128)(2,1)} collective-permute-done((bf16[1024,384]{1,0:T(8,128)(2,1)}, bf16[1024,384]{1,0:T(8,128)(2,1)}, u32[]{:S(2)}, u32[]{:S(2)}) %collective-permute-start.10) | collective-permute-done | bytes 786464 | tf_op jit(solution)/shard_map/ppermute | solution.py:25
  28.1 50.7 %all_to_all.37 = s32[4,8,2]{1,2,0:T(2,128)S(1)} all-to-all(s32[4,8,2]{1,2,0:T(2,128)S(1)} %copy.9), channel_id=1, replica_groups=mesh['grid'=32,'layer'=4] {'layer'}, dimensions={0} | all-to-all | bytes 512 | tf_op jit(solution)/shard_map/all_to_all | solution.py:68
  98.9 26.7 %collective-permute-done.17 = bf16[1024,384]{1,0:T(8,128)(2,1)} collective-permute-done((bf16[1024,384]{1,0:T(8,128)(2,1)}, bf16[1024,384]{1,0:T(8,128)(2,1)}, u32[]{:S(2)}, u32[]{:S(2)}) %collective-permute-start.17) | collective-permute-done | bytes 786464 | tf_op jit(solution)/shard_map/ppermute | solution.py:28
  127.6 16.0 %collective-permute-done.16 = bf16[1024,384]{1,0:T(8,128)(2,1)} collective-permute-done((bf16[1024,384]{1,0:T(8,128)(2,1)}, bf16[1024,384]{1,0:T(8,128)(2,1)}, u32[]{:S(2)}, u32[]{:S(2)}) %collective-permute-start.16) | collective-permute-done | bytes 786464 | tf_op jit(solution)/shard_map/ppermute | solution.py:25
  156.4 5.1 %collective-permute-start.14 = (bf16[256,384]{1,0:T(8,128)(2,1)}, bf16[256,384]{1,0:T(8,128)(2,1)}, u32[]{:S(2)}, u32[]{:S(2)}) collective-permute-start(bf16[256,384]{1,0:T(8,128)(2,1)} %get-tuple-element.31), channel_id=1, source_target_pairs={{4,0},{8,4},{12,8},{16,12},{20,16},{24,20},{28,24},{32,28},{36,32}... | collective-permute-start | bytes 589832 | tf_op jit(solution)/shard_map/ppermute | solution.py:48
  171.1 5.1 %collective-permute-start.19 = (bf16[256,384]{1,0:T(8,128)(2,1)}, bf16[256,384]{1,0:T(8,128)(2,1)}, u32[]{:S(2)}, u32[]{:S(2)}) collective-permute-start(bf16[256,384]{1,0:T(8,128)(2,1)} %get-tuple-element.33), channel_id=1, source_target_pairs={{4,0},{8,4},{12,8},{16,12},{20,16},{24,20},{28,24},{32,28},{36,32}... | collective-permute-start | bytes 589832 | tf_op jit(solution)/shard_map/ppermute | solution.py:48
  185.6 5.1 %collective-permute-start.9 = (bf16[256,384]{1,0:T(8,128)(2,1)S(1)}, bf16[256,384]{1,0:T(8,128)(2,1)S(1)}, u32[]{:S(2)}, u32[]{:S(2)}) collective-permute-start(bf16[256,384]{1,0:T(8,128)(2,1)S(1)} %copy-done.15), channel_id=1, source_target_pairs={{4,0},{8,4},{12,8},{16,12},{20,16},{24,20},{28,24},{32,28},{36,32}... | collective-permute-start | bytes 589832 | tf_op jit(solution)/shard_map/ppermute | solution.py:48
  195.9 6.1 %gather_fusion.5 = bf16[64,128,384]{2,1,0:T(8,128)(2,1)} fusion(bf16[36,128,384]{2,1,0:T(8,128)(2,1)} %bitcast.178, s32[1024]{0:T(1024)S(1)} %pad_clamp_fusion), kind=kCustom, calls=%fused_computation.5 | custom fusion | bytes 12583168 | tf_op jit(solution)/shard_map/gather | solution.py:57
  212.0 6.1 %gather_fusion.7 = bf16[64,128,384]{2,1,0:T(8,128)(2,1)} fusion(bf16[36,128,384]{2,1,0:T(8,128)(2,1)} %bitcast.179, s32[1024]{0:T(1024)S(1)} %pad_clamp_fusion), kind=kCustom, calls=%fused_computation.7 | custom fusion | bytes 12583168 | tf_op jit(solution)/shard_map/gather | solution.py:57
  218.1 5.3 %bitcast_multiply_fusion.5 = f32[8,384,128]{1,2,0:T(8,128)} fusion(bf16[8,8,128,128]{3,2,1,0:T(8,128)(2,1)S(1)} %bitcast.161, bf16[8,8,128,384]{3,2,1,0:T(8,128)(2,1)} %bitcast.169), kind=kOutput, calls=%fused_computation.55 | convolution fusion | flops 805699584 | bytes 9961472 | tf_op jit(solution)/shard_map/rsij,rsjc->ric/dot_general | solution.py:58
  225.9 6.3 %pad_maximum_fusion.1 = bf16[4608,384]{1,0:T(8,128)(2,1)} fusion(bf16[256,384]{1,0:T(8,128)(2,1)S(1)} %collective-permute-done.9, bf16[4096,384]{1,0:T(8,128)(2,1)S(1)} %bitcast.194, bf16[256,384]{1,0:T(8,128)(2,1)S(1)} %collective-permute-done.8), kind=kLoop, calls=%fused_computation.17 | loop fusion | flops 10616832 | bytes 7077888 | tf_op jit(solution)/shard_map/concatenate | solution.py:49
  232.2 6.1 %gather_fusion.3 = bf16[64,128,384]{2,1,0:T(8,128)(2,1)} fusion(bf16[36,128,384]{2,1,0:T(8,128)(2,1)} %bitcast.180, s32[1024]{0:T(1024)S(1)} %pad_clamp_fusion), kind=kCustom, calls=%fused_computation.3 | custom fusion | bytes 12583168 | tf_op jit(solution)/shard_map/gather | solution.py:57
  238.3 5.3 %bitcast_multiply_fusion.6 = f32[8,384,128]{1,2,0:T(8,128)} fusion(bf16[8,8,128,128]{3,2,1,0:T(8,128)(2,1)S(1)} %bitcast.163, bf16[8,8,128,384]{3,2,1,0:T(8,128)(2,1)} %bitcast.172), kind=kOutput, calls=%fused_computation.56 | convolution fusion | flops 805699584 | bytes 9961472 | tf_op jit(solution)/shard_map/rsij,rsjc->ric/dot_general | solution.py:58
  243.6 6.5 %pad_maximum_fusion = bf16[4608,384]{1,0:T(8,128)(2,1)} fusion(bf16[256,384]{1,0:T(8,128)(2,1)S(1)} %collective-permute-done.4, bf16[4096,384]{1,0:T(8,128)(2,1)S(1)} %bitcast.200, bf16[256,384]{1,0:T(8,128)(2,1)S(1)} %collective-permute-done.3), kind=kLoop, calls=%fused_computation.16 | loop fusion | flops 10616832 | bytes 7077888 | tf_op jit(solution)/shard_map/concatenate | solution.py:49
  250.1 6.1 %gather_fusion.1 = bf16[64,128,384]{2,1,0:T(8,128)(2,1)} fusion(bf16[36,128,384]{2,1,0:T(8,128)(2,1)} %bitcast.181, s32[1024]{0:T(1024)S(1)} %pad_clamp_fusion), kind=kCustom, calls=%fused_computation.1 | custom fusion | bytes 12583168 | tf_op jit(solution)/shard_map/gather | solution.py:57
  266.5 18.4 %collective-permute-done.35 = bf16[1024,384]{1,0:T(8,128)(2,1)S(1)} collective-permute-done((bf16[1024,384]{1,0:T(8,128)(2,1)S(1)}, bf16[1024,384]{1,0:T(8,128)(2,1)S(1)}, u32[]{:S(2)}, u32[]{:S(2)}) %collective-permute-start.35) | collective-permute-done | bytes 786464 | tf_op jit(solution)/shard_map/ppermute | solution.py:25
  288.1 13.7 %collective-permute-done.30 = bf16[1024,384]{1,0:T(8,128)(2,1)} collective-permute-done((bf16[1024,384]{1,0:T(8,128)(2,1)}, bf16[1024,384]{1,0:T(8,128)(2,1)}, u32[]{:S(2)}, u32[]{:S(2)}) %collective-permute-start.30) | collective-permute-done | bytes 786464 | tf_op jit(solution)/shard_map/ppermute | solution.py:25
  304.7 13.9 %collective-permute-done.25 = bf16[1024,384]{1,0:T(8,128)(2,1)} collective-permute-done((bf16[1024,384]{1,0:T(8,128)(2,1)}, bf16[1024,384]{1,0:T(8,128)(2,1)}, u32[]{:S(2)}, u32[]{:S(2)}) %collective-permute-start.25) | collective-permute-done | bytes 786464 | tf_op jit(solution)/shard_map/ppermute | solution.py:25
  318.7 16.7 %collective-permute-done.36 = bf16[1024,384]{1,0:T(8,128)(2,1)S(1)} collective-permute-done((bf16[1024,384]{1,0:T(8,128)(2,1)S(1)}, bf16[1024,384]{1,0:T(8,128)(2,1)S(1)}, u32[]{:S(2)}, u32[]{:S(2)}) %collective-permute-start.36) | collective-permute-done | bytes 786464 | tf_op jit(solution)/shard_map/ppermute | solution.py:25
  346.9 5.5 %collective-permute-done.20 = bf16[1024,384]{1,0:T(8,128)(2,1)} collective-permute-done((bf16[1024,384]{1,0:T(8,128)(2,1)S(1)}, bf16[1024,384]{1,0:T(8,128)(2,1)}, u32[]{:S(2)}, u32[]{:S(2)}) %collective-permute-start.20) | collective-permute-done | bytes 786464 | tf_op jit(solution)/shard_map/ppermute | solution.py:25
  352.4 16.8 %collective-permute-done.31 = bf16[1024,384]{1,0:T(8,128)(2,1)} collective-permute-done((bf16[1024,384]{1,0:T(8,128)(2,1)}, bf16[1024,384]{1,0:T(8,128)(2,1)}, u32[]{:S(2)}, u32[]{:S(2)}) %collective-permute-start.31) | collective-permute-done | bytes 786464 | tf_op jit(solution)/shard_map/ppermute | solution.py:25
  395.8 5.1 %collective-permute-start.34 = (bf16[256,384]{1,0:T(8,128)(2,1)}, bf16[256,384]{1,0:T(8,128)(2,1)}, u32[]{:S(2)}, u32[]{:S(2)}) collective-permute-start(bf16[256,384]{1,0:T(8,128)(2,1)} %get-tuple-element.11), channel_id=1, source_target_pairs={{4,0},{8,4},{12,8},{16,12},{20,16},{24,20},{28,24},{32,28},{36,32}... | collective-permute-start | bytes 589832 | tf_op jit(solution)/shard_map/ppermute | solution.py:48
  410.3 5.1 %collective-permute-start.29 = (bf16[256,384]{1,0:T(8,128)(2,1)S(1)}, bf16[256,384]{1,0:T(8,128)(2,1)S(1)}, u32[]{:S(2)}, u32[]{:S(2)}) collective-permute-start(bf16[256,384]{1,0:T(8,128)(2,1)S(1)} %copy-done.16), channel_id=1, source_target_pairs={{4,0},{8,4},{12,8},{16,12},{20,16},{24,20},{28,24},{32,28},{36,32}... | collective-permute-start | bytes 589832 | tf_op jit(solution)/shard_map/ppermute | solution.py:48
  420.4 6.1 %gather_fusion.15 = bf16[64,128,384]{2,1,0:T(8,128)(2,1)} fusion(bf16[36,128,384]{2,1,0:T(8,128)(2,1)} %bitcast.182, s32[1024]{0:T(1024)S(1)} %pad_clamp_fusion), kind=kCustom, calls=%fused_computation.15 | custom fusion | bytes 12583168 | tf_op jit(solution)/shard_map/gather | solution.py:57
  426.4 5.4 %bitcast_multiply_fusion = f32[8,384,128]{1,2,0:T(8,128)} fusion(bf16[8,8,128,128]{3,2,1,0:T(8,128)(2,1)S(1)} %bitcast.165, bf16[8,8,128,384]{3,2,1,0:T(8,128)(2,1)} %bitcast.174), kind=kOutput, calls=%fused_computation.50 | convolution fusion | flops 805699584 | bytes 9961472 | tf_op jit(solution)/shard_map/rsij,rsjc->ric/dot_general | solution.py:58
  441.2 6.1 %gather_fusion.13 = bf16[64,128,384]{2,1,0:T(8,128)(2,1)} fusion(bf16[36,128,384]{2,1,0:T(8,128)(2,1)} %bitcast.183, s32[1024]{0:T(1024)S(1)} %pad_clamp_fusion), kind=kCustom, calls=%fused_computation.13 | custom fusion | bytes 12583168 | tf_op jit(solution)/shard_map/gather | solution.py:57
  447.3 5.3 %bitcast_multiply_fusion.1 = f32[8,384,128]{1,2,0:T(8,128)} fusion(bf16[8,8,128,128]{3,2,1,0:T(8,128)(2,1)S(1)} %bitcast.166, bf16[8,8,128,384]{3,2,1,0:T(8,128)(2,1)} %bitcast.175), kind=kOutput, calls=%fused_computation.51 | convolution fusion | flops 805699584 | bytes 9961472 | tf_op jit(solution)/shard_map/rsij,rsjc->ric/dot_general | solution.py:58
  452.6 6.3 %pad_maximum_fusion.5 = bf16[4608,384]{1,0:T(8,128)(2,1)} fusion(bf16[256,384]{1,0:T(8,128)(2,1)S(1)} %collective-permute-done.29, bf16[4096,384]{1,0:T(8,128)(2,1)S(1)} %bitcast.196, bf16[256,384]{1,0:T(8,128)(2,1)S(1)} %collective-permute-done.28), kind=kLoop, calls=%fused_computation.21 | loop fusion | flops 10616832 | bytes 7077888 | tf_op jit(solution)/shard_map/concatenate | solution.py:49
  458.9 6.1 %gather_fusion.11 = bf16[64,128,384]{2,1,0:T(8,128)(2,1)} fusion(bf16[36,128,384]{2,1,0:T(8,128)(2,1)} %bitcast.184, s32[1024]{0:T(1024)S(1)} %pad_clamp_fusion), kind=kCustom, calls=%fused_computation.11 | custom fusion | bytes 12583168 | tf_op jit(solution)/shard_map/gather | solution.py:57
  465.0 5.3 %bitcast_multiply_fusion.2 = f32[8,384,128]{1,2,0:T(8,128)} fusion(bf16[8,8,128,128]{3,2,1,0:T(8,128)(2,1)S(1)} %bitcast.167, bf16[8,8,128,384]{3,2,1,0:T(8,128)(2,1)} %bitcast.176), kind=kOutput, calls=%fused_computation.52 | convolution fusion | flops 805699584 | bytes 9961472 | tf_op jit(solution)/shard_map/rsij,rsjc->ric/dot_general | solution.py:58
  470.3 6.5 %pad_maximum_fusion.4 = bf16[4608,384]{1,0:T(8,128)(2,1)} fusion(bf16[256,384]{1,0:T(8,128)(2,1)S(1)} %collective-permute-done.24, bf16[4096,384]{1,0:T(8,128)(2,1)S(1)} %bitcast.198, bf16[256,384]{1,0:T(8,128)(2,1)S(1)} %collective-permute-done.23), kind=kLoop, calls=%fused_computation.20 | loop fusion | flops 10616832 | bytes 7077888 | tf_op jit(solution)/shard_map/concatenate | solution.py:49
  476.8 6.1 %gather_fusion.9 = bf16[64,128,384]{2,1,0:T(8,128)(2,1)} fusion(bf16[36,128,384]{2,1,0:T(8,128)(2,1)} %bitcast.177, s32[1024]{0:T(1024)S(1)} %pad_clamp_fusion), kind=kCustom, calls=%fused_computation.9 | custom fusion | bytes 12583168 | tf_op jit(solution)/shard_map/gather | solution.py:57
  (150 shorter events, 168.1 us)
Async XLA Ops:
  7.1 78.5 %collective-permute-start.12 = (bf16[1024,384]{1,0:T(8,128)(2,1)}, bf16[1024,384]{1,0:T(8,128)(2,1)}, u32[]{:S(2)}, u32[]{:S(2)}) collective-permute-start(bf16[1024,384]{1,0:T(8,128)(2,1)} %get-tuple-element.27), channel_id=1, source_target_pairs={{1,0},{2,1},{3,2},{0,3},{5,4},{6,5},{7,6},{4,7},{9,8},{10,9},{11,1... | collective-permute-start | bytes 2359304 | tf_op jit(solution)/shard_map/ppermute | solution.py:28
  9.3 76.4 %collective-permute-start.15 = (bf16[1024,384]{1,0:T(8,128)(2,1)}, bf16[1024,384]{1,0:T(8,128)(2,1)}, u32[]{:S(2)}, u32[]{:S(2)}) collective-permute-start(bf16[1024,384]{1,0:T(8,128)(2,1)} %get-tuple-element.26), channel_id=1, source_target_pairs={{0,1},{1,2},{2,3},{3,0},{4,5},{5,6},{6,7},{7,4},{8,9},{9,10},{10,1... | collective-permute-start | bytes 2359304 | tf_op jit(solution)/shard_map/ppermute | solution.py:25
  9.3 77.4 %collective-permute-start.5 = (bf16[1024,384]{1,0:T(8,128)(2,1)}, bf16[1024,384]{1,0:T(8,128)(2,1)}, u32[]{:S(2)}, u32[]{:S(2)}) collective-permute-start(bf16[1024,384]{1,0:T(8,128)(2,1)} %get-tuple-element.24), channel_id=1, source_target_pairs={{0,1},{1,2},{2,3},{3,0},{4,5},{5,6},{6,7},{7,4},{8,9},{9,10},{10,1... | collective-permute-start | bytes 2359304 | tf_op jit(solution)/shard_map/ppermute | solution.py:25
  27.9 61.3 %collective-permute-start.11 = (bf16[1024,384]{1,0:T(8,128)(2,1)}, bf16[1024,384]{1,0:T(8,128)(2,1)}, u32[]{:S(2)}, u32[]{:S(2)}) collective-permute-start(bf16[1024,384]{1,0:T(8,128)(2,1)} %collective-permute-done.10), channel_id=1, source_target_pairs={{0,1},{1,2},{2,3},{3,0},{4,5},{5,6},{6,7},{7,4},{8,9},{9,10},{10,1... | collective-permute-start | bytes 2359304 | tf_op jit(solution)/shard_map/ppermute | solution.py:25
  78.8 68.1 %all-to-all-start.1 = ((bf16[32,2,128,128]{3,2,1,0:T(8,128)(2,1)}), bf16[32,2,128,128]{3,2,1,0:T(8,128)(2,1)S(1)}, u32[]{:S(2)}, u32[]{:S(2)}) async-start(bf16[32,2,128,128]{3,2,1,0:T(8,128)(2,1)} %param.4), calls=%async_computation.1 | async-start | bytes 4194304 | tf_op jit(solution)/shard_map/all_to_all | solution.py:67
  82.4 43.2 %collective-permute-start.17 = (bf16[1024,384]{1,0:T(8,128)(2,1)}, bf16[1024,384]{1,0:T(8,128)(2,1)}, u32[]{:S(2)}, u32[]{:S(2)}) collective-permute-start(bf16[1024,384]{1,0:T(8,128)(2,1)} %get-tuple-element.26), channel_id=1, source_target_pairs={{1,0},{2,1},{3,2},{0,3},{5,4},{6,5},{7,6},{4,7},{9,8},{10,9},{11,1... | collective-permute-start | bytes 2359304 | tf_op jit(solution)/shard_map/ppermute | solution.py:28
  85.6 41.2 %collective-permute-start = (bf16[1024,384]{1,0:T(8,128)(2,1)}, bf16[1024,384]{1,0:T(8,128)(2,1)}, u32[]{:S(2)}, u32[]{:S(2)}) collective-permute-start(bf16[1024,384]{1,0:T(8,128)(2,1)} %get-tuple-element.25), channel_id=1, source_target_pairs={{0,1},{1,2},{2,3},{3,0},{4,5},{5,6},{6,7},{7,4},{8,9},{9,10},{10,1... | collective-permute-start | bytes 2359304 | tf_op jit(solution)/shard_map/ppermute | solution.py:25
  85.7 57.9 %collective-permute-start.16 = (bf16[1024,384]{1,0:T(8,128)(2,1)}, bf16[1024,384]{1,0:T(8,128)(2,1)}, u32[]{:S(2)}, u32[]{:S(2)}) collective-permute-start(bf16[1024,384]{1,0:T(8,128)(2,1)} %collective-permute-done.15), channel_id=1, source_target_pairs={{0,1},{1,2},{2,3},{3,0},{4,5},{5,6},{6,7},{7,4},{8,9},{9,10},{10,1... | collective-permute-start | bytes 2359304 | tf_op jit(solution)/shard_map/ppermute | solution.py:25
  86.7 69.7 %collective-permute-start.7 = (bf16[1024,384]{1,0:T(8,128)(2,1)}, bf16[1024,384]{1,0:T(8,128)(2,1)}, u32[]{:S(2)}, u32[]{:S(2)}) collective-permute-start(bf16[1024,384]{1,0:T(8,128)(2,1)} %get-tuple-element.24), channel_id=1, source_target_pairs={{1,0},{2,1},{3,2},{0,3},{5,4},{6,5},{7,6},{4,7},{9,8},{10,9},{11,1... | collective-permute-start | bytes 2359304 | tf_op jit(solution)/shard_map/ppermute | solution.py:28
  89.3 72.2 %collective-permute-start.6 = (bf16[1024,384]{1,0:T(8,128)(2,1)}, bf16[1024,384]{1,0:T(8,128)(2,1)}, u32[]{:S(2)}, u32[]{:S(2)}) collective-permute-start(bf16[1024,384]{1,0:T(8,128)(2,1)} %collective-permute-done.5), channel_id=1, source_target_pairs={{0,1},{1,2},{2,3},{3,0},{4,5},{5,6},{6,7},{7,4},{8,9},{9,10},{10,1... | collective-permute-start | bytes 2359304 | tf_op jit(solution)/shard_map/ppermute | solution.py:25
  125.6 45.5 %collective-permute-start.2 = (bf16[1024,384]{1,0:T(8,128)(2,1)}, bf16[1024,384]{1,0:T(8,128)(2,1)}, u32[]{:S(2)}, u32[]{:S(2)}) collective-permute-start(bf16[1024,384]{1,0:T(8,128)(2,1)} %get-tuple-element.25), channel_id=1, source_target_pairs={{1,0},{2,1},{3,2},{0,3},{5,4},{6,5},{7,6},{4,7},{9,8},{10,9},{11,1... | collective-permute-start | bytes 2359304 | tf_op jit(solution)/shard_map/ppermute | solution.py:28
  126.8 49.4 %collective-permute-start.1 = (bf16[1024,384]{1,0:T(8,128)(2,1)}, bf16[1024,384]{1,0:T(8,128)(2,1)}, u32[]{:S(2)}, u32[]{:S(2)}) collective-permute-start(bf16[1024,384]{1,0:T(8,128)(2,1)} %collective-permute-done), channel_id=1, source_target_pairs={{0,1},{1,2},{2,3},{3,0},{4,5},{5,6},{6,7},{7,4},{8,9},{9,10},{10,1... | collective-permute-start | bytes 2359304 | tf_op jit(solution)/shard_map/ppermute | solution.py:25
  143.6 42.0 %collective-permute-start.13 = (bf16[256,384]{1,0:T(8,128)(2,1)}, bf16[256,384]{1,0:T(8,128)(2,1)S(1)}, u32[]{:S(2)}, u32[]{:S(2)}) collective-permute-start(bf16[256,384]{1,0:T(8,128)(2,1)} %get-tuple-element.30), channel_id=1, source_target_pairs={{0,4},{4,8},{8,12},{12,16},{16,20},{20,24},{24,28},{28,32},{32,36}... | collective-permute-start | bytes 589832 | tf_op jit(solution)/shard_map/ppermute | solution.py:47
  161.5 40.4 %collective-permute-start.18 = (bf16[256,384]{1,0:T(8,128)(2,1)}, bf16[256,384]{1,0:T(8,128)(2,1)S(1)}, u32[]{:S(2)}, u32[]{:S(2)}) collective-permute-start(bf16[256,384]{1,0:T(8,128)(2,1)} %get-tuple-element.32), channel_id=1, source_target_pairs={{0,4},{4,8},{8,12},{12,16},{16,20},{20,24},{24,28},{28,32},{32,36}... | collective-permute-start | bytes 589832 | tf_op jit(solution)/shard_map/ppermute | solution.py:47
  176.1 49.8 %collective-permute-start.8 = (bf16[256,384]{1,0:T(8,128)(2,1)}, bf16[256,384]{1,0:T(8,128)(2,1)S(1)}, u32[]{:S(2)}, u32[]{:S(2)}) collective-permute-start(bf16[256,384]{1,0:T(8,128)(2,1)} %get-tuple-element.28), channel_id=1, source_target_pairs={{0,4},{4,8},{8,12},{12,16},{16,20},{20,24},{24,28},{28,32},{32,36}... | collective-permute-start | bytes 589832 | tf_op jit(solution)/shard_map/ppermute | solution.py:47
  190.7 52.9 %collective-permute-start.3 = (bf16[256,384]{1,0:T(8,128)(2,1)}, bf16[256,384]{1,0:T(8,128)(2,1)S(1)}, u32[]{:S(2)}, u32[]{:S(2)}) collective-permute-start(bf16[256,384]{1,0:T(8,128)(2,1)} %get-tuple-element.18), channel_id=1, source_target_pairs={{0,4},{4,8},{8,12},{12,16},{16,20},{20,24},{24,28},{28,32},{32,36}... | collective-permute-start | bytes 589832 | tf_op jit(solution)/shard_map/ppermute | solution.py:47
  201.9 41.7 %collective-permute-start.4 = (bf16[256,384]{1,0:T(8,128)(2,1)S(1)}, bf16[256,384]{1,0:T(8,128)(2,1)S(1)}, u32[]{:S(2)}, u32[]{:S(2)}) collective-permute-start(bf16[256,384]{1,0:T(8,128)(2,1)S(1)} %get-tuple-element.19), channel_id=1, source_target_pairs={{4,0},{8,4},{12,8},{16,12},{20,16},{24,20},{28,24},{32,28},{36,32}... | collective-permute-start | bytes 589832 | tf_op jit(solution)/shard_map/ppermute | solution.py:48
  266.5 52.2 %collective-permute-start.25 = (bf16[1024,384]{1,0:T(8,128)(2,1)}, bf16[1024,384]{1,0:T(8,128)(2,1)}, u32[]{:S(2)}, u32[]{:S(2)}) collective-permute-start(bf16[1024,384]{1,0:T(8,128)(2,1)} %get-tuple-element.15), channel_id=1, source_target_pairs={{0,1},{1,2},{2,3},{3,0},{4,5},{5,6},{6,7},{7,4},{8,9},{9,10},{10,1... | collective-permute-start | bytes 2359304 | tf_op jit(solution)/shard_map/ppermute | solution.py:25
  284.9 50.6 %collective-permute-start.36 = (bf16[1024,384]{1,0:T(8,128)(2,1)S(1)}, bf16[1024,384]{1,0:T(8,128)(2,1)S(1)}, u32[]{:S(2)}, u32[]{:S(2)}) collective-permute-start(bf16[1024,384]{1,0:T(8,128)(2,1)S(1)} %collective-permute-done.35), channel_id=1, source_target_pairs={{0,1},{1,2},{2,3},{3,0},{4,5},{5,6},{6,7},{7,4},{8,9},{9,10},{10,1... | collective-permute-start | bytes 2359304 | tf_op jit(solution)/shard_map/ppermute | solution.py:25
  284.9 58.8 %collective-permute-start.32 = (bf16[1024,384]{1,0:T(8,128)(2,1)}, bf16[1024,384]{1,0:T(8,128)(2,1)}, u32[]{:S(2)}, u32[]{:S(2)}) collective-permute-start(bf16[1024,384]{1,0:T(8,128)(2,1)} %get-tuple-element.17), channel_id=1, source_target_pairs={{1,0},{2,1},{3,2},{0,3},{5,4},{6,5},{7,6},{4,7},{9,8},{10,9},{11,1... | collective-permute-start | bytes 2359304 | tf_op jit(solution)/shard_map/ppermute | solution.py:28
  288.1 64.3 %collective-permute-start.20 = (bf16[1024,384]{1,0:T(8,128)(2,1)S(1)}, bf16[1024,384]{1,0:T(8,128)(2,1)}, u32[]{:S(2)}, u32[]{:S(2)}) collective-permute-start(bf16[1024,384]{1,0:T(8,128)(2,1)S(1)} %get-tuple-element.14), channel_id=1, source_target_pairs={{0,1},{1,2},{2,3},{3,0},{4,5},{5,6},{6,7},{7,4},{8,9},{9,10},{10,1... | collective-permute-start | bytes 2359304 | tf_op jit(solution)/shard_map/ppermute | solution.py:25
  301.8 67.4 %collective-permute-start.31 = (bf16[1024,384]{1,0:T(8,128)(2,1)}, bf16[1024,384]{1,0:T(8,128)(2,1)}, u32[]{:S(2)}, u32[]{:S(2)}) collective-permute-start(bf16[1024,384]{1,0:T(8,128)(2,1)} %collective-permute-done.30), channel_id=1, source_target_pairs={{0,1},{1,2},{2,3},{3,0},{4,5},{5,6},{6,7},{7,4},{8,9},{9,10},{10,1... | collective-permute-start | bytes 2359304 | tf_op jit(solution)/shard_map/ppermute | solution.py:25
  318.7 60.6 %collective-permute-start.27 = (bf16[1024,384]{1,0:T(8,128)(2,1)}, bf16[1024,384]{1,0:T(8,128)(2,1)}, u32[]{:S(2)}, u32[]{:S(2)}) collective-permute-start(bf16[1024,384]{1,0:T(8,128)(2,1)} %get-tuple-element.15), channel_id=1, source_target_pairs={{1,0},{2,1},{3,2},{0,3},{5,4},{6,5},{7,6},{4,7},{9,8},{10,9},{11,1... | collective-permute-start | bytes 2359304 | tf_op jit(solution)/shard_map/ppermute | solution.py:28
  335.4 50.7 %collective-permute-start.26 = (bf16[1024,384]{1,0:T(8,128)(2,1)}, bf16[1024,384]{1,0:T(8,128)(2,1)}, u32[]{:S(2)}, u32[]{:S(2)}) collective-permute-start(bf16[1024,384]{1,0:T(8,128)(2,1)} %collective-permute-done.25), channel_id=1, source_target_pairs={{0,1},{1,2},{2,3},{3,0},{4,5},{5,6},{6,7},{7,4},{8,9},{9,10},{10,1... | collective-permute-start | bytes 2359304 | tf_op jit(solution)/shard_map/ppermute | solution.py:25
  343.7 52.1 %collective-permute-start.22 = (bf16[1024,384]{1,0:T(8,128)(2,1)S(1)}, bf16[1024,384]{1,0:T(8,128)(2,1)}, u32[]{:S(2)}, u32[]{:S(2)}) collective-permute-start(bf16[1024,384]{1,0:T(8,128)(2,1)S(1)} %get-tuple-element.14), channel_id=1, source_target_pairs={{1,0},{2,1},{3,2},{0,3},{5,4},{6,5},{7,6},{4,7},{9,8},{10,9},{11,1... | collective-permute-start | bytes 2359304 | tf_op jit(solution)/shard_map/ppermute | solution.py:28
  352.4 48.5 %collective-permute-start.21 = (bf16[1024,384]{1,0:T(8,128)(2,1)}, bf16[1024,384]{1,0:T(8,128)(2,1)}, u32[]{:S(2)}, u32[]{:S(2)}) collective-permute-start(bf16[1024,384]{1,0:T(8,128)(2,1)} %collective-permute-done.20), channel_id=1, source_target_pairs={{0,1},{1,2},{2,3},{3,0},{4,5},{5,6},{6,7},{7,4},{8,9},{9,10},{10,1... | collective-permute-start | bytes 2359304 | tf_op jit(solution)/shard_map/ppermute | solution.py:25
  369.2 41.1 %collective-permute-start.38 = (bf16[256,384]{1,0:T(8,128)(2,1)}, bf16[256,384]{1,0:T(8,128)(2,1)S(1)}, u32[]{:S(2)}, u32[]{:S(2)}) collective-permute-start(bf16[256,384]{1,0:T(8,128)(2,1)} %get-tuple-element.12), channel_id=1, source_target_pairs={{0,4},{4,8},{8,12},{12,16},{16,20},{20,24},{24,28},{28,32},{32,36}... | collective-permute-start | bytes 589832 | tf_op jit(solution)/shard_map/ppermute | solution.py:47
  386.1 45.7 %collective-permute-start.33 = (bf16[256,384]{1,0:T(8,128)(2,1)}, bf16[256,384]{1,0:T(8,128)(2,1)S(1)}, u32[]{:S(2)}, u32[]{:S(2)}) collective-permute-start(bf16[256,384]{1,0:T(8,128)(2,1)} %get-tuple-element.10), channel_id=1, source_target_pairs={{0,4},{4,8},{8,12},{12,16},{16,20},{20,24},{24,28},{28,32},{32,36}... | collective-permute-start | bytes 589832 | tf_op jit(solution)/shard_map/ppermute | solution.py:47
  395.8 41.1 %collective-permute-start.34 = (bf16[256,384]{1,0:T(8,128)(2,1)}, bf16[256,384]{1,0:T(8,128)(2,1)}, u32[]{:S(2)}, u32[]{:S(2)}) collective-permute-start(bf16[256,384]{1,0:T(8,128)(2,1)} %get-tuple-element.11), channel_id=1, source_target_pairs={{4,0},{8,4},{12,8},{16,12},{20,16},{24,20},{28,24},{32,28},{36,32}... | collective-permute-start | bytes 589832 | tf_op jit(solution)/shard_map/ppermute | solution.py:48
  400.9 51.7 %collective-permute-start.28 = (bf16[256,384]{1,0:T(8,128)(2,1)}, bf16[256,384]{1,0:T(8,128)(2,1)S(1)}, u32[]{:S(2)}, u32[]{:S(2)}) collective-permute-start(bf16[256,384]{1,0:T(8,128)(2,1)} %get-tuple-element.8), channel_id=1, source_target_pairs={{0,4},{4,8},{8,12},{12,16},{16,20},{20,24},{24,28},{28,32},{32,36}... | collective-permute-start | bytes 589832 | tf_op jit(solution)/shard_map/ppermute | solution.py:47
  410.3 42.3 %collective-permute-start.29 = (bf16[256,384]{1,0:T(8,128)(2,1)S(1)}, bf16[256,384]{1,0:T(8,128)(2,1)S(1)}, u32[]{:S(2)}, u32[]{:S(2)}) collective-permute-start(bf16[256,384]{1,0:T(8,128)(2,1)S(1)} %copy-done.16), channel_id=1, source_target_pairs={{4,0},{8,4},{12,8},{16,12},{20,16},{24,20},{28,24},{32,28},{36,32}... | collective-permute-start | bytes 589832 | tf_op jit(solution)/shard_map/ppermute | solution.py:48
  415.4 55.0 %collective-permute-start.23 = (bf16[256,384]{1,0:T(8,128)(2,1)}, bf16[256,384]{1,0:T(8,128)(2,1)S(1)}, u32[]{:S(2)}, u32[]{:S(2)}) collective-permute-start(bf16[256,384]{1,0:T(8,128)(2,1)} %get-tuple-element.6), channel_id=1, source_target_pairs={{0,4},{4,8},{8,12},{12,16},{16,20},{20,24},{24,28},{28,32},{32,36}... | collective-permute-start | bytes 589832 | tf_op jit(solution)/shard_map/ppermute | solution.py:47
  (27 other events, 401.4 us)
